TPU v7x, 128 devices: a whole 4x4x4 slice. The times are simulated.
128 devices in a mesh: dp: 8 (over x, core), eig: 16 (over y, z).
Axes of the slice: x: 4, y: 4, z: 4, core: 2. Of those that a mesh axis runs over, the one named last changes fastest.
Arguments:
- acts: bfloat16 [4096, 8192], P(('dp', 'eig')), may hold values from -6 to 6
- grads: bfloat16 [4096, 8192], P(('dp', 'eig')), may hold values from -6 to 6
- act_basis: bfloat16 [4096, 8192], P('eig'), may hold values from -0.0625 to 0.0625
- grad_basis: bfloat16 [4096, 8192], P('eig'), may hold values from -0.0625 to 0.0625
- eigenvalues: float32 [4096, 4096], P('eig'), may hold values from 0.05 to 20
- query_grads: bfloat16 [32, 256, 4096], P('dp', None, 'eig'), may hold values from -6 to 6
- query_acts: bfloat16 [32, 256, 4096], P('dp'), may hold values from -6 to 6
- cand_local: int32 [8, 16], P('dp'), may hold values from 0 to 7, as said below
- seq_lengths: int32 [8, 8], P('dp'), may hold values from 1 to 128, 512 in all within a row
Outputs:
- scores: float32 [32, 16], P('dp')
Inputs may be any that keep to these rules, and one draw needn't show every extreme that they name: `cand_local`: entry j of an owner's list names a sequence of dp shard j // 2; the 2 entries of one list that name one shard differ. `seq_lengths`: row d lists the lengths of the 8 sequences packed in order in dp shard d's 512 token rows; they sum to 512.
All inputs are finite; a program needn't handle non-finite values.
Results may differ from a plain program's by a relative error of at most 0.006.
Values may be sent and summed in bfloat16 or wider, within the bound.
No kernel may reach another device: no remote copies, remote signals or barrier semaphores. Data moves between devices by JAX's collectives and lax.ppermute only.
A program may use at most 128 MiB of HBM per device.

v0:
```python
import math
import jax
import jax.numpy as jnp
from jax import lax
from jax.sharding import PartitionSpec as P

DAMPING = 0.1


def shards(
    acts,
    grads,
    act_basis,
    grad_basis,
    eigenvalues,
    query_grads,
    query_acts,
    cand_local,
    seq_lengths,
):
    block_width = act_basis.shape[0]
    queries = query_grads.shape[0]
    full_width = query_acts.shape[2]
    seq_count = seq_lengths.shape[1]
    group_rows = acts.shape[0] * lax.axis_size("eig")
    max_len = 2 * group_rows // seq_count
    pick_lists = lax.all_to_all(cand_local, "dp", split_axis=1, concat_axis=0, tiled=True)
    owners = pick_lists.shape[0]
    per_shard = pick_lists.shape[1]
    lengths = seq_lengths[0]
    offsets = jnp.cumsum(lengths) - lengths
    chosen = (
        pick_lists[:, :, None] == jnp.arange(seq_count, dtype=jnp.int32)[None, None, :]
    ).astype(jnp.int32)
    pick_len = jnp.sum(chosen * lengths[None, None, :], axis=2)
    pick_start = jnp.sum(chosen * offsets[None, None, :], axis=2)
    within = jnp.arange(max_len, dtype=jnp.int32)
    is_live = within[None, None, :] < pick_len[:, :, None]
    row_index = jnp.where(is_live, pick_start[:, :, None] + within[None, None, :], -1).reshape(-1)
    select = (row_index[:, None] == jnp.arange(group_rows, dtype=jnp.int32)[None, :]).astype(
        jnp.bfloat16
    )

    def rotate_and_pack(rows, basis):
        shard_rows = lax.all_gather(rows, "eig", axis=0, tiled=True)
        rotated = jnp.dot(shard_rows, basis.T, preferred_element_type=jnp.float32).astype(
            jnp.bfloat16
        )
        rotated = lax.optimization_barrier(rotated)
        packed = jnp.dot(select, rotated, preferred_element_type=jnp.float32).astype(jnp.bfloat16)
        packed = packed.reshape(owners, per_shard * max_len, block_width)
        return lax.all_to_all(packed, "dp", split_axis=0, concat_axis=0, tiled=True)

    act_narrow = rotate_and_pack(acts, act_basis)
    act_recv = lax.all_gather(act_narrow, "eig", axis=2, tiled=True)
    grad_recv = rotate_and_pack(grads, grad_basis)
    slot_count = owners * per_shard * max_len
    grad_flat = grad_recv.reshape(slot_count, block_width).astype(jnp.float32)
    act_flat = act_recv.reshape(slot_count, full_width)
    damped = eigenvalues + DAMPING
    query_outer = jnp.einsum(
        "qti,qtk->qik", query_grads, query_acts, preferred_element_type=jnp.float32
    )
    precond = (query_outer / damped[None]).astype(jnp.bfloat16)
    precond = lax.optimization_barrier(precond.reshape(queries * block_width, full_width))
    projected = lax.dot_general(
        act_flat, precond, (((1,), (1,)), ((), ())), preferred_element_type=jnp.float32
    )
    projected = lax.optimization_barrier(projected).reshape(slot_count, queries, block_width)
    per_token = jnp.sum(projected * grad_flat[:, None, :], axis=2)
    partial_sums = jnp.sum(per_token.reshape(owners * per_shard, max_len, queries), axis=1).T
    summed = lax.psum(partial_sums, "eig")
    score_scale = 1.0 / (full_width * 4.0 * math.sqrt(query_acts.shape[1]))
    return summed * score_scale


def solution(mesh):
    placed = (
        P(("dp", "eig"), None),
        P(("dp", "eig"), None),
        P("eig", None),
        P("eig", None),
        P("eig", None),
        P("dp", None, "eig"),
        P("dp", None, None),
        P("dp", None),
        P("dp", None),
    )
    return jax.shard_map(
        shards, mesh=mesh, in_specs=placed, out_specs=P("dp", None), check_vma=False
    )
```

profile of v0, /device:TPU:0, one launch (start us, length us, event | category | flops | bytes accessed | tf_op | source)
XLA Modules:
  0.0 363.8 jit_solution(16105542730583716110)
XLA Ops:
  6.5 0.7 all-gather.4.cloned.1.call-update
  8.5 1.3 reduce.3
  10.5 4.4 %all-to-all-start = ((s32[1,8,2]{2,0,1:T(1,128)}), s32[1,8,2]{2,0,1:T(1,128)S(1)}, u32[]{:S(2)}, u32[]{:S(2)}) async-start(s32[1,8,2]{2,0,1:T(1,128)} %bitcast), calls=%async_computation | async-start | bytes 8192 | tf_op jit(solution)/shard_map/all_to_all | solution.py:27
  15.0 0.8 reduce-window.8
  16.5 3.7 %all-to-all-done = s32[1,8,2]{2,0,1:T(1,128)S(1)} async-done(((s32[1,8,2]{2,0,1:T(1,128)}), s32[1,8,2]{2,0,1:T(1,128)S(1)}, u32[]{:S(2)}, u32[]{:S(2)}) %all-to-all-start) | async-done | bytes 96 | tf_op jit(solution)/shard_map/all_to_all | solution.py:27
  20.3 0.9 select_reduce_fusion.1
  21.4 61.6 %all-gather.4.cloned.1.call-done = bf16[512,8192]{1,0:T(8,128)(2,1)} async-done(((bf16[32,8192]{1,0:T(8,128)(2,1)}), bf16[512,8192]{1,0:T(8,128)(2,1)}) %all-gather.4.cloned.1.call-update) | async-done | bytes 8388624 | tf_op jit(solution)/shard_map/all_gather | solution.py:45
  83.0 6.9 %convolution_convert_fusion.1 = bf16[512,256]{1,0:T(8,128)(2,1)S(1)} fusion(bf16[512,8192]{1,0:T(8,128)(2,1)} %all-gather.4.cloned.1.call-done, bf16[256,8192]{1,0:T(8,128)(2,1)} %param.11), kind=kOutput, calls=%fused_computation.11 | convolution fusion | flops 2147614720 | bytes 12845056 | tf_op jit(solution)/shard_map/dot_general | solution.py:46
  89.9 1.1 fusion.2
  91.0 20.1 %all_to_all.23 = bf16[8,256,256]{2,1,0:T(8,128)(2,1)} all-to-all(bf16[8,256,256]{2,1,0:T(8,128)(2,1)S(1)} %bitcast.28), channel_id=1, replica_groups=mesh['dp'=8,'eig'=16] {'dp'}, dimensions={0} | all-to-all | bytes 2097152 | tf_op jit(solution)/shard_map/all_to_all | solution.py:52
  111.2 4.8 %broadcast_add_fusion = f32[256,4096]{1,0:T(8,128)} fusion(f32[256,4096]{1,0:T(8,128)} %param.13), kind=kLoop, calls=%fused_computation.7 | loop fusion | flops 1048576 | bytes 8388608 | tf_op jit(solution)/shard_map/add | solution.py:60
  115.9 39.8 %all-gather.8.cloned.1.call-done = bf16[512,8192]{1,0:T(8,128)(2,1)} async-done(((bf16[32,8192]{1,0:T(8,128)(2,1)}), bf16[512,8192]{1,0:T(8,128)(2,1)}) %all-gather.8.cloned.1.call-update) | async-done | bytes 8388624 | tf_op jit(solution)/shard_map/all_gather | solution.py:45
  155.7 6.9 %convolution_convert_fusion = bf16[512,256]{1,0:T(8,128)(2,1)S(1)} fusion(bf16[512,8192]{1,0:T(8,128)(2,1)} %all-gather.8.cloned.1.call-done, bf16[256,8192]{1,0:T(8,128)(2,1)} %param.12), kind=kOutput, calls=%fused_computation.10 | convolution fusion | flops 2147614720 | bytes 12845056 | tf_op jit(solution)/shard_map/dot_general | solution.py:46
  162.6 1.9 fusion.3
  164.5 4.3 %all-to-all-start.2 = ((bf16[8,256,256]{2,1,0:T(8,128)(2,1)}), bf16[8,256,256]{2,1,0:T(8,128)(2,1)S(1)}, u32[]{:S(2)}, u32[]{:S(2)}) async-start(bf16[8,256,256]{2,1,0:T(8,128)(2,1)} %bitcast.9), calls=%async_computation.2 | async-start | bytes 2097152 | tf_op jit(solution)/shard_map/all_to_all | solution.py:52
  168.7 9.2 %divide_convert_fusion = bf16[4,256,4096]{2,1,0:T(8,128)(2,1)} fusion(f32[256,4096]{1,0:T(8,128)} %broadcast_add_fusion, bf16[4,256,256]{2,1,0:T(8,128)(2,1)S(1)} %copy-done, bf16[4,256,4096]{2,1,0:T(8,128)(2,1)} %param.15), kind=kOutput, calls=%fused_computation | convolution fusion | flops 2155872256 | bytes 21495808 | tf_op jit(solution)/shard_map/qti,qtk->qik/dot_general | solution.py:61
  177.9 6.7 %all-to-all-done.2 = bf16[8,256,256]{2,1,0:T(8,128)(2,1)S(1)} async-done(((bf16[8,256,256]{2,1,0:T(8,128)(2,1)}), bf16[8,256,256]{2,1,0:T(8,128)(2,1)S(1)}, u32[]{:S(2)}, u32[]{:S(2)}) %all-to-all-start.2) | async-done | bytes 1048608 | tf_op jit(solution)/shard_map/all_to_all | solution.py:52
  184.7 1.1 copy-done.2
  185.7 1.4 convert.1
  187.1 90.2 %all-gather.6.cloned.1.call-done = bf16[8,256,4096]{2,1,0:T(8,128)(2,1)} async-done(((bf16[8,256,256]{2,1,0:T(8,128)(2,1)}), bf16[8,256,4096]{2,1,0:T(8,128)(2,1)}) %all-gather.6.cloned.1.call-update) | async-done | bytes 16777232 | tf_op jit(solution)/shard_map/all_gather | solution.py:55
  277.4 24.1 %fusion.6 = f32[2048,1024]{1,0:T(8,128)} fusion(bf16[2048,4096]{1,0:T(8,128)(2,1)} %bitcast.35, bf16[1024,4096]{1,0:T(8,128)(2,1)} %bitcast.36), kind=kOutput, calls=%fused_computation.19 | convolution fusion | flops 17179869184 | bytes 33554432 | tf_op jit(solution)/shard_map/dot_general | solution.py:66
  301.5 10.6 %reshape.106 = f32[2048,4,256]{2,1,0:T(4,128)} reshape(f32[2048,1024]{1,0:T(8,128)} %fusion.6) | data formatting | bytes 16777216 | tf_op jit(solution)/shard_map/reshape | solution.py:69
  312.1 6.3 %multiply_reduce_fusion = f32[2048,4]{1,0:T(8,128)S(1)} fusion(f32[2048,4,256]{2,1,0:T(4,128)} %reshape.106, f32[2048,256]{1,0:T(8,128)S(1)} %convert.1), kind=kLoop, calls=%fused_computation.1 | loop fusion | flops 4186112 | bytes 10518528 | tf_op jit(solution)/shard_map/reduce_sum | solution.py:70
  318.6 38.1 %psum.7 = f32[4,16]{1,0:T(4,128)S(1)} all-reduce(f32[4,16]{1,0:T(4,128)S(1)} %bitcast.29), channel_id=1, replica_groups=mesh['dp'=8,'eig'=16] {'eig'}, use_global_device_ids=true, to_apply=%region_5.6 | all-reduce | flops 64 | bytes 512 | tf_op jit(solution)/shard_map/psum | solution.py:72
  (20 shorter events, 3.7 us)
Async XLA Ops:
  6.5 162.2 %copy-start = (bf16[4,256,256]{2,1,0:T(8,128)(2,1)S(1)}, bf16[4,256,256]{2,1,0:T(8,128)(2,1)}, u32[]{:S(2)}) copy-start(bf16[4,256,256]{2,1,0:T(8,128)(2,1)} %param.14) | copy-start | bytes 1572868
  6.5 76.4 %all-gather.4.cloned.1.call-start = ((), (), s32[]{:S(2)}) async-start(), calls=%async_computation.3 | async-start | bytes 8912896 | tf_op jit(solution)/shard_map/all_gather | solution.py:45
  7.3 148.4 %all-gather.8.cloned.1.call-start = ((), (), s32[]{:S(2)}) async-start(), calls=%async_computation.5 | async-start | bytes 8912896 | tf_op jit(solution)/shard_map/all_gather | solution.py:45
  10.5 9.7 %all-to-all-start = ((s32[1,8,2]{2,0,1:T(1,128)}), s32[1,8,2]{2,0,1:T(1,128)S(1)}, u32[]{:S(2)}, u32[]{:S(2)}) async-start(s32[1,8,2]{2,0,1:T(1,128)} %bitcast), calls=%async_computation | async-start | bytes 8192 | tf_op jit(solution)/shard_map/all_to_all | solution.py:27
  14.9 262.5 %all-gather.6.cloned.1.call-start = ((), (), s32[]{:S(2)}) async-start(), calls=%async_computation.4 | async-start | bytes 17825792 | tf_op jit(solution)/shard_map/all_gather | solution.py:55
  164.5 20.2 %all-to-all-start.2 = ((bf16[8,256,256]{2,1,0:T(8,128)(2,1)}), bf16[8,256,256]{2,1,0:T(8,128)(2,1)S(1)}, u32[]{:S(2)}, u32[]{:S(2)}) async-start(bf16[8,256,256]{2,1,0:T(8,128)(2,1)} %bitcast.9), calls=%async_computation.2 | async-start | bytes 2097152 | tf_op jit(solution)/shard_map/all_to_all | solution.py:52
  184.7 1.1 copy-start.2
  301.5 55.8 %copy-start.1 = (bf16[4,256,256]{2,1,0:T(8,128)(2,1)S(1)}, bf16[4,256,256]{2,1,0:T(8,128)(2,1)}, u32[]{:S(2)}) copy-start(bf16[4,256,256]{2,1,0:T(8,128)(2,1)} %param.14) | copy-start | bytes 1572868
Sparse Core Ops, SparseCore 0:
  9.5 73.4 all-gather.3
  85.1 70.4 all-gather.7
  157.8 119.5 all-gather.5
where the time goes:
time: 364 us
  waiting for transfers between devices  203 us (56%)
  blocking collectives  58.3 us (16%)
  matrix products  50.1 us (14%)
  other arithmetic  16.9 us (5%)
  local copies, waits for them, and re-layouts  13.2 us (4%)
  between operations  13.2 us (4%)
  starting transfers between devices  8.75 us (2%)
    all_gather x2, waiting for transfers between devices, rotate_and_pack(): shard_rows = lax.all_gather(rows, 'eig', axis=0, tiled=True)  101 us
    all_gather x1, waiting for transfers between devices, shards(): act_recv = lax.all_gather(act_narrow, 'eig', axis=2, tiled=True)  90.2 us
    psum x1, blocking collectives, shards(): summed = lax.psum(partial_sums, 'eig')  38.1 us
    dot_general x1, matrix products, shards(): lax.dot_general(act_flat, precond, (((1,), (1,)), ((), ())), preferred_el...  24.1 us
    all_to_all x1, blocking collectives, rotate_and_pack(): return lax.all_to_all(packed, 'dp', split_axis=0, concat_axis=0, tiled=True)  20.1 us
    dot_general x2, matrix products, rotate_and_pack(): jnp.dot(shard_rows, basis.T, preferred_element_type=jnp.float32)  13.9 us
    reshape x1, local copies, waits for them, and re-layouts, shards(): lax.optimization_barrier(projected)  10.6 us
    dot_general x1, matrix products, shards(): jnp.einsum('qti,qtk->qik', query_grads, query_acts, preferred_element_typ...  9.21 us
  transfers between devices with their start and end apart: 5, of which 5 were waited for; matrix products, arithmetic and copies ran while one was open for 10% of the time, Pallas kernels for 0%

commit v1 on v0

--- a/solution.py
+++ b/solution.py
@@ -52,7 +52,22 @@
         return lax.all_to_all(packed, "dp", split_axis=0, concat_axis=0, tiled=True)
 
     act_narrow = rotate_and_pack(acts, act_basis)
-    act_recv = lax.all_gather(act_narrow, "eig", axis=2, tiled=True)
+    ways, here, step = (lax.axis_size("eig"), lax.axis_index("eig"), act_narrow.shape[2])
+    shape = [n * ways if d == 2 else n for d, n in enumerate(act_narrow.shape)]
+    act_recv = lax.dynamic_update_slice_in_dim(
+        jnp.zeros(shape, act_narrow.dtype), act_narrow, here * step, axis=2
+    )
+    going_up = going_down = act_narrow
+    for far in range(1, ways // 2 + 1):
+        going_up = lax.ppermute(going_up, "eig", [(d, (d + 1) % ways) for d in range(ways)])
+        act_recv = lax.dynamic_update_slice_in_dim(
+            act_recv, going_up, (here - far) % ways * step, axis=2
+        )
+        if 2 * far < ways:
+            going_down = lax.ppermute(going_down, "eig", [(d, (d - 1) % ways) for d in range(ways)])
+            act_recv = lax.dynamic_update_slice_in_dim(
+                act_recv, going_down, (here + far) % ways * step, axis=2
+            )
     grad_recv = rotate_and_pack(grads, grad_basis)
     slot_count = owners * per_shard * max_len
     grad_flat = grad_recv.reshape(slot_count, block_width).astype(jnp.float32)

time: 364 us -> 434 us (1.19)
  starting transfers between devices: 8.75 us -> 46.1 us
  local copies, waits for them, and re-layouts: 13.2 us -> 32.2 us
  waiting for transfers between devices: 203 us -> 222 us
    ppermute x0 -> x15, waiting for transfers between devices: none -> 155 us  [the longest x8 141 us: shards(): lax.ppermute(going_up, 'eig', [(d, (d + 1) % ways) for d in range(ways)])]
    all_gather x1 -> x0, waiting for transfers between devices: 90.2 us -> none  [shards(): act_recv = lax.all_gather(act_narrow, 'eig', axis=2, tiled=True)]
    all_gather x2, waiting for transfers between devices: 101 us -> 61.6 us  [rotate_and_pack(): shard_rows = lax.all_gather(rows, 'eig', axis=0, tiled=True)]
    ppermute x0 -> x15, starting transfers between devices: none -> 38 us  [the longest x7 36.5 us: shards(): lax.ppermute(going_down, 'eig', [(d, (d - 1) % ways) for d in range(ways)])]
    dynamic_update_slice x0 -> x16, local copies, waits for them, and re-layouts: none -> 17 us  [the longest x8 8.49 us: shards(): lax.dynamic_update_slice_in_dim(act_recv, going_up, (here - far) % ways *...]
    all_to_all x1, waiting for transfers between devices: 6.71 us -> 0.01 us  [rotate_and_pack(): return lax.all_to_all(packed, 'dp', split_axis=0, concat_axis=0, tiled=True)]
  transfers between devices with their start and end apart: 5 -> 19, of which waited for: 5 -> 11; matrix products, arithmetic and copies ran while one was open for 10% -> 12% of each run, Pallas kernels for 0% -> 0%
where the time goes in v1:
time: 434 us; the launch traced here: 433 us
  waiting for transfers between devices  222 us (51%)
  blocking collectives  55.6 us (13%)
  matrix products  49.5 us (11%)
  starting transfers between devices  46.1 us (11%)
  local copies, waits for them, and re-layouts  32.2 us (7%)
  other arithmetic  14.6 us (3%)
  between operations  13.7 us (3%)
    ppermute x8, waiting for transfers between devices, shards(): lax.ppermute(going_up, 'eig', [(d, (d + 1) % ways) for d in range(ways)])  141 us
    all_gather x2, waiting for transfers between devices, rotate_and_pack(): shard_rows = lax.all_gather(rows, 'eig', axis=0, tiled=True)  61.6 us
    ppermute x7, starting transfers between devices, shards(): lax.ppermute(going_down, 'eig', [(d, (d - 1) % ways) for d in range(ways)])  36.5 us
    psum x1, blocking collectives, shards(): summed = lax.psum(partial_sums, 'eig')  35.4 us
    dot_general x1, matrix products, shards(): lax.dot_general(act_flat, precond, (((1,), (1,)), ((), ())), preferred_el...  23.5 us
    all_to_all x1, blocking collectives, rotate_and_pack(): return lax.all_to_all(packed, 'dp', split_axis=0, concat_axis=0, tiled=True)  20.1 us
    dot_general x2, matrix products, rotate_and_pack(): jnp.dot(shard_rows, basis.T, preferred_element_type=jnp.float32)  14 us
    ppermute x7, waiting for transfers between devices, shards(): lax.ppermute(going_down, 'eig', [(d, (d - 1) % ways) for d in range(ways)])  13.7 us
  transfers between devices with their start and end apart: 19, of which 11 were waited for; matrix products, arithmetic and copies ran while one was open for 12% of the time, Pallas kernels for 0%

profile of v1, /device:TPU:0, one launch (start us, length us, event | category | flops | bytes accessed | tf_op | source)
XLA Modules:
  0.0 433.5 jit_solution(8152148257108456582)
XLA Ops:
  10.5 4.4 %all-to-all-start = ((s32[1,8,2]{2,0,1:T(1,128)}), s32[1,8,2]{2,0,1:T(1,128)S(1)}, u32[]{:S(2)}, u32[]{:S(2)}) async-start(s32[1,8,2]{2,0,1:T(1,128)} %bitcast), calls=%async_computation | async-start | bytes 8192 | tf_op jit(solution)/shard_map/all_to_all | solution.py:27
  21.4 61.6 %all-gather.3.cloned.1.call-done = bf16[512,8192]{1,0:T(8,128)(2,1)} async-done(((bf16[32,8192]{1,0:T(8,128)(2,1)}), bf16[512,8192]{1,0:T(8,128)(2,1)}) %all-gather.3.cloned.1.call-update) | async-done | bytes 8388624 | tf_op jit(solution)/shard_map/all_gather | solution.py:45
  83.0 7.1 %convolution_convert_fusion.1 = bf16[512,256]{1,0:T(8,128)(2,1)S(1)} fusion(bf16[512,8192]{1,0:T(8,128)(2,1)} %all-gather.3.cloned.1.call-done, bf16[256,8192]{1,0:T(8,128)(2,1)} %param.11), kind=kOutput, calls=%fused_computation.11 | convolution fusion | flops 2147614720 | bytes 12845056 | tf_op jit(solution)/shard_map/dot_general | solution.py:46
  91.2 20.1 %all_to_all.23 = bf16[8,256,256]{2,1,0:T(8,128)(2,1)} all-to-all(bf16[8,256,256]{2,1,0:T(8,128)(2,1)S(1)} %bitcast.30), channel_id=1, replica_groups=mesh['dp'=8,'eig'=16] {'dp'}, dimensions={0} | all-to-all | bytes 2097152 | tf_op jit(solution)/shard_map/all_to_all | solution.py:52
  116.6 39.8 %collective-permute-done = bf16[8,256,256]{2,1,0:T(8,128)(2,1)S(1)} collective-permute-done((bf16[8,256,256]{2,1,0:T(8,128)(2,1)}, bf16[8,256,256]{2,1,0:T(8,128)(2,1)S(1)}, u32[]{:S(2)}, u32[]{:S(2)}) %collective-permute-start) | collective-permute-done | bytes 1048608 | tf_op jit(solution)/shard_map/ppermute | solution.py:62
  161.1 5.7 %collective-permute-start.3 = (bf16[8,256,256]{2,1,0:T(8,128)(2,1)S(1)}, bf16[8,256,256]{2,1,0:T(8,128)(2,1)S(1)}, u32[]{:S(2)}, u32[]{:S(2)}) collective-permute-start(bf16[8,256,256]{2,1,0:T(8,128)(2,1)S(1)} %collective-permute-done.1), channel_id=1, source_target_pairs={{0,15},{1,0},{2,1},{3,2},{4,3},{5,4},{6,5},{7,6},{8,7},{9,8},{10,9... | collective-permute-start | bytes 3145736 | tf_op jit(solution)/shard_map/ppermute | solution.py:67
  166.8 28.7 %collective-permute-done.2 = bf16[8,256,256]{2,1,0:T(8,128)(2,1)S(1)} collective-permute-done((bf16[8,256,256]{2,1,0:T(8,128)(2,1)S(1)}, bf16[8,256,256]{2,1,0:T(8,128)(2,1)S(1)}, u32[]{:S(2)}, u32[]{:S(2)}) %collective-permute-start.2) | collective-permute-done | bytes 1048608 | tf_op jit(solution)/shard_map/ppermute | solution.py:62
  195.6 5.3 %collective-permute-start.5 = (bf16[8,256,256]{2,1,0:T(8,128)(2,1)S(1)}, bf16[8,256,256]{2,1,0:T(8,128)(2,1)S(1)}, u32[]{:S(2)}, u32[]{:S(2)}) collective-permute-start(bf16[8,256,256]{2,1,0:T(8,128)(2,1)S(1)} %collective-permute-done.3), channel_id=1, source_target_pairs={{0,15},{1,0},{2,1},{3,2},{4,3},{5,4},{6,5},{7,6},{8,7},{9,8},{10,9... | collective-permute-start | bytes 3145736 | tf_op jit(solution)/shard_map/ppermute | solution.py:67
  200.9 21.4 %collective-permute-done.4 = bf16[8,256,256]{2,1,0:T(8,128)(2,1)S(1)} collective-permute-done((bf16[8,256,256]{2,1,0:T(8,128)(2,1)S(1)}, bf16[8,256,256]{2,1,0:T(8,128)(2,1)S(1)}, u32[]{:S(2)}, u32[]{:S(2)}) %collective-permute-start.4) | collective-permute-done | bytes 1048608 | tf_op jit(solution)/shard_map/ppermute | solution.py:62
  222.3 5.3 %collective-permute-start.7 = (bf16[8,256,256]{2,1,0:T(8,128)(2,1)S(1)}, bf16[8,256,256]{2,1,0:T(8,128)(2,1)S(1)}, u32[]{:S(2)}, u32[]{:S(2)}) collective-permute-start(bf16[8,256,256]{2,1,0:T(8,128)(2,1)S(1)} %collective-permute-done.5), channel_id=1, source_target_pairs={{0,15},{1,0},{2,1},{3,2},{4,3},{5,4},{6,5},{7,6},{8,7},{9,8},{10,9... | collective-permute-start | bytes 3145736 | tf_op jit(solution)/shard_map/ppermute | solution.py:67
  227.6 20.5 %collective-permute-done.6 = bf16[8,256,256]{2,1,0:T(8,128)(2,1)S(1)} collective-permute-done((bf16[8,256,256]{2,1,0:T(8,128)(2,1)S(1)}, bf16[8,256,256]{2,1,0:T(8,128)(2,1)S(1)}, u32[]{:S(2)}, u32[]{:S(2)}) %collective-permute-start.6) | collective-permute-done | bytes 1048608 | tf_op jit(solution)/shard_map/ppermute | solution.py:62
  250.6 5.4 %collective-permute-start.9 = (bf16[8,256,256]{2,1,0:T(8,128)(2,1)S(1)}, bf16[8,256,256]{2,1,0:T(8,128)(2,1)}, u32[]{:S(2)}, u32[]{:S(2)}) collective-permute-start(bf16[8,256,256]{2,1,0:T(8,128)(2,1)S(1)} %collective-permute-done.7), channel_id=1, source_target_pairs={{0,15},{1,0},{2,1},{3,2},{4,3},{5,4},{6,5},{7,6},{8,7},{9,8},{10,9... | collective-permute-start | bytes 3145736 | tf_op jit(solution)/shard_map/ppermute | solution.py:67
  256.0 17.4 %collective-permute-done.8 = bf16[8,256,256]{2,1,0:T(8,128)(2,1)} collective-permute-done((bf16[8,256,256]{2,1,0:T(8,128)(2,1)S(1)}, bf16[8,256,256]{2,1,0:T(8,128)(2,1)}, u32[]{:S(2)}, u32[]{:S(2)}) %collective-permute-start.8) | collective-permute-done | bytes 1048608 | tf_op jit(solution)/shard_map/ppermute | solution.py:62
  273.5 6.9 %convolution_convert_fusion = bf16[512,256]{1,0:T(8,128)(2,1)S(1)} fusion(bf16[512,8192]{1,0:T(8,128)(2,1)} %all-gather.5.cloned.1.call-done, bf16[256,8192]{1,0:T(8,128)(2,1)} %param.12), kind=kOutput, calls=%fused_computation.10 | convolution fusion | flops 2147614720 | bytes 12845056 | tf_op jit(solution)/shard_map/dot_general | solution.py:46
  285.9 5.4 %collective-permute-start.11 = (bf16[8,256,256]{2,1,0:T(8,128)(2,1)}, bf16[8,256,256]{2,1,0:T(8,128)(2,1)}, u32[]{:S(2)}, u32[]{:S(2)}) collective-permute-start(bf16[8,256,256]{2,1,0:T(8,128)(2,1)} %collective-permute-done.9), channel_id=1, source_target_pairs={{0,15},{1,0},{2,1},{3,2},{4,3},{5,4},{6,5},{7,6},{8,7},{9,8},{10,9... | collective-permute-start | bytes 3145736 | tf_op jit(solution)/shard_map/ppermute | solution.py:67
  291.3 6.7 %collective-permute-done.10 = bf16[8,256,256]{2,1,0:T(8,128)(2,1)} collective-permute-done((bf16[8,256,256]{2,1,0:T(8,128)(2,1)}, bf16[8,256,256]{2,1,0:T(8,128)(2,1)}, u32[]{:S(2)}, u32[]{:S(2)}) %collective-permute-start.10) | collective-permute-done | bytes 1048608 | tf_op jit(solution)/shard_map/ppermute | solution.py:62
  297.9 9.1 %divide_convert_fusion = bf16[4,256,4096]{2,1,0:T(8,128)(2,1)} fusion(f32[256,4096]{1,0:T(8,128)} %broadcast_add_fusion, bf16[4,256,256]{2,1,0:T(8,128)(2,1)S(1)} %copy-done, bf16[4,256,4096]{2,1,0:T(8,128)(2,1)} %param.15), kind=kOutput, calls=%fused_computation | convolution fusion | flops 2155872256 | bytes 21495808 | tf_op jit(solution)/shard_map/qti,qtk->qik/dot_general | solution.py:76
  318.7 5.4 %collective-permute-start.13 = (bf16[8,256,256]{2,1,0:T(8,128)(2,1)}, bf16[8,256,256]{2,1,0:T(8,128)(2,1)S(1)}, u32[]{:S(2)}, u32[]{:S(2)}) collective-permute-start(bf16[8,256,256]{2,1,0:T(8,128)(2,1)} %collective-permute-done.11), channel_id=1, source_target_pairs={{0,15},{1,0},{2,1},{3,2},{4,3},{5,4},{6,5},{7,6},{8,7},{9,8},{10,9... | collective-permute-start | bytes 3145736 | tf_op jit(solution)/shard_map/ppermute | solution.py:67
  332.8 10.1 %collective-permute-done.13 = bf16[8,256,256]{2,1,0:T(8,128)(2,1)S(1)} collective-permute-done((bf16[8,256,256]{2,1,0:T(8,128)(2,1)}, bf16[8,256,256]{2,1,0:T(8,128)(2,1)S(1)}, u32[]{:S(2)}, u32[]{:S(2)}) %collective-permute-start.13) | collective-permute-done | bytes 1048608 | tf_op jit(solution)/shard_map/ppermute | solution.py:67
  343.0 6.7 %collective-permute-done.14 = bf16[8,256,256]{2,1,0:T(8,128)(2,1)S(1)} collective-permute-done((bf16[8,256,256]{2,1,0:T(8,128)(2,1)}, bf16[8,256,256]{2,1,0:T(8,128)(2,1)S(1)}, u32[]{:S(2)}, u32[]{:S(2)}) %collective-permute-start.14) | collective-permute-done | bytes 1048608 | tf_op jit(solution)/shard_map/ppermute | solution.py:62
  349.9 23.5 %fusion.6 = f32[2048,1024]{1,0:T(8,128)} fusion(bf16[2048,4096]{1,0:T(8,128)(2,1)S(1)} %bitcast.27, bf16[1024,4096]{1,0:T(8,128)(2,1)} %bitcast.37), kind=kOutput, calls=%fused_computation.35 | convolution fusion | flops 17179869184 | bytes 33554432 | tf_op jit(solution)/shard_map/dot_general | solution.py:81
  373.4 10.8 %reshape.106 = f32[2048,4,256]{2,1,0:T(4,128)} reshape(f32[2048,1024]{1,0:T(8,128)} %fusion.6) | data formatting | bytes 16777216 | tf_op jit(solution)/shard_map/reshape | solution.py:84
  384.2 6.3 %multiply_reduce_fusion = f32[2048,4]{1,0:T(8,128)S(1)} fusion(f32[2048,4,256]{2,1,0:T(4,128)} %reshape.106, f32[2048,256]{1,0:T(8,128)S(1)} %copy-done.2), kind=kLoop, calls=%fused_computation.1 | loop fusion | flops 4186112 | bytes 10518528 | tf_op jit(solution)/shard_map/reduce_sum | solution.py:85
  390.6 35.4 %psum.7 = f32[4,16]{1,0:T(4,128)S(1)} all-reduce(f32[4,16]{1,0:T(4,128)S(1)} %bitcast.31), channel_id=1, replica_groups=mesh['dp'=8,'eig'=16] {'eig'}, use_global_device_ids=true, to_apply=%region_5.6 | all-reduce | flops 64 | bytes 512 | tf_op jit(solution)/shard_map/psum | solution.py:87
  (86 shorter events, 50.7 us)
Async XLA Ops:
  6.5 291.4 %copy-start = (bf16[4,256,256]{2,1,0:T(8,128)(2,1)S(1)}, bf16[4,256,256]{2,1,0:T(8,128)(2,1)}, u32[]{:S(2)}) copy-start(bf16[4,256,256]{2,1,0:T(8,128)(2,1)} %param.14) | copy-start | bytes 1572868
  6.5 76.4 %all-gather.3.cloned.1.call-start = ((), (), s32[]{:S(2)}) async-start(), calls=%async_computation.3 | async-start | bytes 8912896 | tf_op jit(solution)/shard_map/all_gather | solution.py:45
  7.3 266.2 %all-gather.5.cloned.1.call-start = ((), (), s32[]{:S(2)}) async-start(), calls=%async_computation.4 | async-start | bytes 8912896 | tf_op jit(solution)/shard_map/all_gather | solution.py:45
  10.5 9.7 %all-to-all-start = ((s32[1,8,2]{2,0,1:T(1,128)}), s32[1,8,2]{2,0,1:T(1,128)S(1)}, u32[]{:S(2)}, u32[]{:S(2)}) async-start(s32[1,8,2]{2,0,1:T(1,128)} %bitcast), calls=%async_computation | async-start | bytes 8192 | tf_op jit(solution)/shard_map/all_to_all | solution.py:27
  83.0 165.3 %copy-start.3 = (f32[256,4096]{1,0:T(8,128)S(1)}, f32[256,4096]{1,0:T(8,128)}, u32[]{:S(2)}) copy-start(f32[256,4096]{1,0:T(8,128)} %param.13) | copy-start | bytes 12582916
  111.3 45.2 %collective-permute-start = (bf16[8,256,256]{2,1,0:T(8,128)(2,1)}, bf16[8,256,256]{2,1,0:T(8,128)(2,1)S(1)}, u32[]{:S(2)}, u32[]{:S(2)}) collective-permute-start(bf16[8,256,256]{2,1,0:T(8,128)(2,1)} %all_to_all.23), channel_id=1, source_target_pairs={{0,1},{1,2},{2,3},{3,4},{4,5},{5,6},{6,7},{7,8},{8,9},{9,10},{10,1... | collective-permute-start | bytes 3145736 | tf_op jit(solution)/shard_map/ppermute | solution.py:62
  112.6 48.4 %collective-permute-start.1 = (bf16[8,256,256]{2,1,0:T(8,128)(2,1)}, bf16[8,256,256]{2,1,0:T(8,128)(2,1)S(1)}, u32[]{:S(2)}, u32[]{:S(2)}) collective-permute-start(bf16[8,256,256]{2,1,0:T(8,128)(2,1)} %all_to_all.23), channel_id=1, source_target_pairs={{0,15},{1,0},{2,1},{3,2},{4,3},{5,4},{6,5},{7,6},{8,7},{9,8},{10,9... | collective-permute-start | bytes 3145736 | tf_op jit(solution)/shard_map/ppermute | solution.py:67
  157.5 38.1 %collective-permute-start.2 = (bf16[8,256,256]{2,1,0:T(8,128)(2,1)S(1)}, bf16[8,256,256]{2,1,0:T(8,128)(2,1)S(1)}, u32[]{:S(2)}, u32[]{:S(2)}) collective-permute-start(bf16[8,256,256]{2,1,0:T(8,128)(2,1)S(1)} %collective-permute-done), channel_id=1, source_target_pairs={{0,1},{1,2},{2,3},{3,4},{4,5},{5,6},{6,7},{7,8},{8,9},{9,10},{10,1... | collective-permute-start | bytes 3145736 | tf_op jit(solution)/shard_map/ppermute | solution.py:62
  161.1 34.5 %collective-permute-start.3 = (bf16[8,256,256]{2,1,0:T(8,128)(2,1)S(1)}, bf16[8,256,256]{2,1,0:T(8,128)(2,1)S(1)}, u32[]{:S(2)}, u32[]{:S(2)}) collective-permute-start(bf16[8,256,256]{2,1,0:T(8,128)(2,1)S(1)} %collective-permute-done.1), channel_id=1, source_target_pairs={{0,15},{1,0},{2,1},{3,2},{4,3},{5,4},{6,5},{7,6},{8,7},{9,8},{10,9... | collective-permute-start | bytes 3145736 | tf_op jit(solution)/shard_map/ppermute | solution.py:67
  195.5 26.8 %collective-permute-start.4 = (bf16[8,256,256]{2,1,0:T(8,128)(2,1)S(1)}, bf16[8,256,256]{2,1,0:T(8,128)(2,1)S(1)}, u32[]{:S(2)}, u32[]{:S(2)}) collective-permute-start(bf16[8,256,256]{2,1,0:T(8,128)(2,1)S(1)} %collective-permute-done.2), channel_id=1, source_target_pairs={{0,1},{1,2},{2,3},{3,4},{4,5},{5,6},{6,7},{7,8},{8,9},{9,10},{10,1... | collective-permute-start | bytes 3145736 | tf_op jit(solution)/shard_map/ppermute | solution.py:62
  195.6 77.9 %copy-start.12 = (bf16[8,256,256]{2,1,0:T(8,128)(2,1)}, bf16[8,256,256]{2,1,0:T(8,128)(2,1)S(1)}, u32[]{:S(2)}) copy-start(bf16[8,256,256]{2,1,0:T(8,128)(2,1)S(1)} %collective-permute-done.3) | copy-start | bytes 3145732
  195.6 26.7 %collective-permute-start.5 = (bf16[8,256,256]{2,1,0:T(8,128)(2,1)S(1)}, bf16[8,256,256]{2,1,0:T(8,128)(2,1)S(1)}, u32[]{:S(2)}, u32[]{:S(2)}) collective-permute-start(bf16[8,256,256]{2,1,0:T(8,128)(2,1)S(1)} %collective-permute-done.3), channel_id=1, source_target_pairs={{0,15},{1,0},{2,1},{3,2},{4,3},{5,4},{6,5},{7,6},{8,7},{9,8},{10,9... | collective-permute-start | bytes 3145736 | tf_op jit(solution)/shard_map/ppermute | solution.py:67
  222.3 25.9 %collective-permute-start.6 = (bf16[8,256,256]{2,1,0:T(8,128)(2,1)S(1)}, bf16[8,256,256]{2,1,0:T(8,128)(2,1)S(1)}, u32[]{:S(2)}, u32[]{:S(2)}) collective-permute-start(bf16[8,256,256]{2,1,0:T(8,128)(2,1)S(1)} %collective-permute-done.4), channel_id=1, source_target_pairs={{0,1},{1,2},{2,3},{3,4},{4,5},{5,6},{6,7},{7,8},{8,9},{9,10},{10,1... | collective-permute-start | bytes 3145736 | tf_op jit(solution)/shard_map/ppermute | solution.py:62
  222.3 28.3 %collective-permute-start.7 = (bf16[8,256,256]{2,1,0:T(8,128)(2,1)S(1)}, bf16[8,256,256]{2,1,0:T(8,128)(2,1)S(1)}, u32[]{:S(2)}, u32[]{:S(2)}) collective-permute-start(bf16[8,256,256]{2,1,0:T(8,128)(2,1)S(1)} %collective-permute-done.5), channel_id=1, source_target_pairs={{0,15},{1,0},{2,1},{3,2},{4,3},{5,4},{6,5},{7,6},{8,7},{9,8},{10,9... | collective-permute-start | bytes 3145736 | tf_op jit(solution)/shard_map/ppermute | solution.py:67
  248.2 25.2 %collective-permute-start.8 = (bf16[8,256,256]{2,1,0:T(8,128)(2,1)S(1)}, bf16[8,256,256]{2,1,0:T(8,128)(2,1)}, u32[]{:S(2)}, u32[]{:S(2)}) collective-permute-start(bf16[8,256,256]{2,1,0:T(8,128)(2,1)S(1)} %collective-permute-done.6), channel_id=1, source_target_pairs={{0,1},{1,2},{2,3},{3,4},{4,5},{5,6},{6,7},{7,8},{8,9},{9,10},{10,1... | collective-permute-start | bytes 3145736 | tf_op jit(solution)/shard_map/ppermute | solution.py:62
  250.6 56.4 %copy-start.9 = (bf16[8,256,256]{2,1,0:T(8,128)(2,1)}, bf16[8,256,256]{2,1,0:T(8,128)(2,1)S(1)}, u32[]{:S(2)}) copy-start(bf16[8,256,256]{2,1,0:T(8,128)(2,1)S(1)} %collective-permute-done.7) | copy-start | bytes 3145732
  250.6 35.2 %collective-permute-start.9 = (bf16[8,256,256]{2,1,0:T(8,128)(2,1)S(1)}, bf16[8,256,256]{2,1,0:T(8,128)(2,1)}, u32[]{:S(2)}, u32[]{:S(2)}) collective-permute-start(bf16[8,256,256]{2,1,0:T(8,128)(2,1)S(1)} %collective-permute-done.7), channel_id=1, source_target_pairs={{0,15},{1,0},{2,1},{3,2},{4,3},{5,4},{6,5},{7,6},{8,7},{9,8},{10,9... | collective-permute-start | bytes 3145736 | tf_op jit(solution)/shard_map/ppermute | solution.py:67
  273.4 24.5 %collective-permute-start.10 = (bf16[8,256,256]{2,1,0:T(8,128)(2,1)}, bf16[8,256,256]{2,1,0:T(8,128)(2,1)}, u32[]{:S(2)}, u32[]{:S(2)}) collective-permute-start(bf16[8,256,256]{2,1,0:T(8,128)(2,1)} %collective-permute-done.8), channel_id=1, source_target_pairs={{0,1},{1,2},{2,3},{3,4},{4,5},{5,6},{6,7},{7,8},{8,9},{9,10},{10,1... | collective-permute-start | bytes 3145736 | tf_op jit(solution)/shard_map/ppermute | solution.py:62
  282.3 24.7 %all-to-all-start.2 = ((bf16[8,256,256]{2,1,0:T(8,128)(2,1)}), bf16[8,256,256]{2,1,0:T(8,128)(2,1)S(1)}, u32[]{:S(2)}, u32[]{:S(2)}) async-start(bf16[8,256,256]{2,1,0:T(8,128)(2,1)} %bitcast.29), calls=%async_computation.2 | async-start | bytes 2097152 | tf_op jit(solution)/shard_map/all_to_all | solution.py:52
  285.9 32.8 %collective-permute-start.11 = (bf16[8,256,256]{2,1,0:T(8,128)(2,1)}, bf16[8,256,256]{2,1,0:T(8,128)(2,1)}, u32[]{:S(2)}, u32[]{:S(2)}) collective-permute-start(bf16[8,256,256]{2,1,0:T(8,128)(2,1)} %collective-permute-done.9), channel_id=1, source_target_pairs={{0,15},{1,0},{2,1},{3,2},{4,3},{5,4},{6,5},{7,6},{8,7},{9,8},{10,9... | collective-permute-start | bytes 3145736 | tf_op jit(solution)/shard_map/ppermute | solution.py:67
  297.9 27.5 %collective-permute-start.12 = (bf16[8,256,256]{2,1,0:T(8,128)(2,1)}, bf16[8,256,256]{2,1,0:T(8,128)(2,1)}, u32[]{:S(2)}, u32[]{:S(2)}) collective-permute-start(bf16[8,256,256]{2,1,0:T(8,128)(2,1)} %collective-permute-done.10), channel_id=1, source_target_pairs={{0,1},{1,2},{2,3},{3,4},{4,5},{5,6},{6,7},{7,8},{8,9},{9,10},{10,1... | collective-permute-start | bytes 3145736 | tf_op jit(solution)/shard_map/ppermute | solution.py:62
  318.7 24.2 %collective-permute-start.13 = (bf16[8,256,256]{2,1,0:T(8,128)(2,1)}, bf16[8,256,256]{2,1,0:T(8,128)(2,1)S(1)}, u32[]{:S(2)}, u32[]{:S(2)}) collective-permute-start(bf16[8,256,256]{2,1,0:T(8,128)(2,1)} %collective-permute-done.11), channel_id=1, source_target_pairs={{0,15},{1,0},{2,1},{3,2},{4,3},{5,4},{6,5},{7,6},{8,7},{9,8},{10,9... | collective-permute-start | bytes 3145736 | tf_op jit(solution)/shard_map/ppermute | solution.py:67
  325.5 24.3 %collective-permute-start.14 = (bf16[8,256,256]{2,1,0:T(8,128)(2,1)}, bf16[8,256,256]{2,1,0:T(8,128)(2,1)S(1)}, u32[]{:S(2)}, u32[]{:S(2)}) collective-permute-start(bf16[8,256,256]{2,1,0:T(8,128)(2,1)} %collective-permute-done.12), channel_id=1, source_target_pairs={{0,1},{1,2},{2,3},{3,4},{4,5},{5,6},{6,7},{7,8},{8,9},{9,10},{10,1... | collective-permute-start | bytes 3145736 | tf_op jit(solution)/shard_map/ppermute | solution.py:62
  349.9 76.8 %copy-start.1 = (bf16[4,256,256]{2,1,0:T(8,128)(2,1)S(1)}, bf16[4,256,256]{2,1,0:T(8,128)(2,1)}, u32[]{:S(2)}) copy-start(bf16[4,256,256]{2,1,0:T(8,128)(2,1)} %param.14) | copy-start | bytes 1572868
  (9 other events, 214.1 us)
Sparse Core Ops, SparseCore 0:
  9.5 73.4 all-gather.2
  85.1 100.6 all-gather.4
